TPU v7x, 128 devices: a whole 4x4x4 slice. The times are simulated.
128 devices in a mesh: dp: 16 (over x, z), fsdp: 8 (over y, core).
Axes of the slice: x: 4, y: 4, z: 4, core: 2. Of those that a mesh axis runs over, the one named last changes fastest.
Arguments:
- tokens: bfloat16 [2048, 4096], P('dp', 'fsdp'), may hold values from -6 to 6
- expert_ids: int32 [2048, 2], P('dp'), may hold values from 0 to 7, all different within a row; in each aligned block of 128 rows (0 to 127, 128 to 255, ...) at most 40 rows name the same one
- route_probs: float32 [2048, 2], P('dp'), may hold values from 0.1 to 0.9
- w_gate: bfloat16 [4096, 65536], P(None, ('dp', 'fsdp')), may hold values from -0.09375 to 0.09375
- w_up: bfloat16 [4096, 65536], P(None, ('dp', 'fsdp')), may hold values from -0.09375 to 0.09375
- w_down: bfloat16 [65536, 4096], P(('dp', 'fsdp')), may hold values from -0.0625 to 0.0625
- out_grad: bfloat16 [2048, 4096], P('dp', 'fsdp'), may hold values from -0.59765625 to 0.59765625
Outputs:
- mixed: bfloat16 [2048, 4096], P('dp', 'fsdp')
- token_grad: bfloat16 [2048, 4096], P('dp', 'fsdp')
- prob_grad: float32 [2048, 2], P('dp')
- gate_weight_grad: bfloat16 [4096, 65536], P(None, ('dp', 'fsdp'))
- up_weight_grad: bfloat16 [4096, 65536], P(None, ('dp', 'fsdp'))
- down_weight_grad: bfloat16 [65536, 4096], P(('dp', 'fsdp'))
Inputs may be any that keep to these rules, and one draw needn't show every extreme that they name: `expert_ids`: each token names two different experts. Within the 128 tokens of one dp index (aligned blocks of rows) no expert is named more than 40 times, and in some block one expert is named exactly 40 times.
All inputs are finite; a program needn't handle non-finite values.
Results may differ from a plain program's by a relative error of at most 0.019.
Values may be sent and summed in bfloat16 or wider, within the bound.
No kernel may reach another device: no remote copies, remote signals or barrier semaphores. Data moves between devices by JAX's collectives and lax.ppermute only.
A program may use at most 128 MiB of HBM per device.

v0:
```python
import jax
import jax.numpy as jnp
from jax import lax
from jax.sharding import PartitionSpec as P

E = 8
CAP = 40


def local(tokens, expert_ids, route_probs, w_gate, w_up, w_down, out_grad):
    dp_count = lax.axis_size("dp")
    groups = dp_count // E
    token_count = tokens.shape[0]
    slot_total = E * CAP
    routing = expert_ids.reshape(-1)
    onehot = (routing[:, None] == jnp.arange(E, dtype=jnp.int32)[None, :]).astype(jnp.int32)
    position = jnp.sum((jnp.cumsum(onehot, axis=0) - onehot) * onehot, axis=1)
    slot_of = (routing * CAP + position).reshape(token_count, 2)
    slot_index = jnp.arange(slot_total, dtype=jnp.int32)
    select_first = slot_of[:, 0:1] == slot_index[None, :]
    select_second = slot_of[:, 1:2] == slot_index[None, :]
    picker = jnp.logical_or(select_first, select_second)
    picker_bf = picker.astype(jnp.bfloat16)
    weighted = jnp.where(select_first, route_probs[:, 0:1], 0.0) + jnp.where(
        select_second, route_probs[:, 1:2], 0.0
    )
    contract_rows = (((0,), (0,)), ((), ()))
    back_dims = (((1,), (1,)), ((), ()))

    def place_rows(source, scaled):
        if scaled:
            placed = lax.dot_general(
                weighted,
                source.astype(jnp.float32),
                contract_rows,
                precision=lax.Precision.HIGHEST,
                preferred_element_type=jnp.float32,
            )
        else:
            placed = lax.dot_general(
                picker_bf, source, contract_rows, preferred_element_type=jnp.float32
            )
        placed = placed.astype(jnp.bfloat16).reshape(E, CAP, source.shape[1])
        return jnp.repeat(placed, groups, axis=0)

    def to_expert_layout(source, scaled):
        joined = lax.all_gather(source, "fsdp", axis=1, tiled=True)
        arrived = lax.all_to_all(
            place_rows(joined, scaled), "dp", split_axis=0, concat_axis=0, tiled=True
        )
        return arrived.reshape(dp_count * CAP, arrived.shape[2])

    def to_token_layout(partial_value):
        shares = lax.psum_scatter(
            partial_value.astype(jnp.bfloat16), "fsdp", scatter_dimension=1, tiled=True
        ).astype(jnp.float32)
        returned = lax.all_to_all(
            shares.reshape(dp_count, CAP, shares.shape[1]).astype(jnp.bfloat16),
            "dp",
            split_axis=0,
            concat_axis=0,
            tiled=True,
        ).astype(jnp.float32)
        return jnp.sum(returned.reshape(E, groups, CAP, returned.shape[2]), axis=1).reshape(
            slot_total, returned.shape[2]
        )

    expert_rows = to_expert_layout(tokens, False)
    gate_proj = jnp.dot(expert_rows, w_gate, preferred_element_type=jnp.float32)
    up_proj = jnp.dot(expert_rows, w_up, preferred_element_type=jnp.float32)
    sigmoid_gate = jax.nn.sigmoid(gate_proj)
    activated = gate_proj * sigmoid_gate
    hidden = (activated * up_proj).astype(jnp.bfloat16)
    out_partial = jnp.dot(hidden, w_down, preferred_element_type=jnp.float32)
    out_slots = to_token_layout(out_partial)
    first_pair = jnp.dot(
        select_first.astype(jnp.float32),
        out_slots,
        precision=lax.Precision.HIGHEST,
        preferred_element_type=jnp.float32,
    )
    second_pair = jnp.dot(
        select_second.astype(jnp.float32),
        out_slots,
        precision=lax.Precision.HIGHEST,
        preferred_element_type=jnp.float32,
    )
    mixed = (route_probs[:, 0:1] * first_pair + route_probs[:, 1:2] * second_pair).astype(
        jnp.bfloat16
    )
    grad_local = out_grad.astype(jnp.float32)
    prob_terms = jnp.stack(
        [jnp.sum(first_pair * grad_local, axis=1), jnp.sum(second_pair * grad_local, axis=1)],
        axis=1,
    )
    prob_grad = lax.psum(prob_terms, "fsdp")
    grad_rows = to_expert_layout(out_grad, True)
    hidden_grad = lax.dot_general(grad_rows, w_down, back_dims, preferred_element_type=jnp.float32)
    gate_grad = (
        hidden_grad * up_proj * sigmoid_gate * (1.0 + gate_proj * (1.0 - sigmoid_gate))
    ).astype(jnp.bfloat16)
    up_grad = (hidden_grad * activated).astype(jnp.bfloat16)
    gate_weight_grad = lax.dot_general(
        expert_rows, gate_grad, contract_rows, preferred_element_type=jnp.float32
    ).astype(jnp.bfloat16)
    up_weight_grad = lax.dot_general(
        expert_rows, up_grad, contract_rows, preferred_element_type=jnp.float32
    ).astype(jnp.bfloat16)
    down_weight_grad = lax.dot_general(
        hidden, grad_rows, contract_rows, preferred_element_type=jnp.float32
    ).astype(jnp.bfloat16)
    input_partial = lax.dot_general(
        gate_grad, w_gate, back_dims, preferred_element_type=jnp.float32
    )
    input_partial = input_partial + lax.dot_general(
        up_grad, w_up, back_dims, preferred_element_type=jnp.float32
    )
    input_slots = to_token_layout(input_partial)
    token_grad = jnp.dot(
        picker.astype(jnp.float32),
        input_slots,
        precision=lax.Precision.HIGHEST,
        preferred_element_type=jnp.float32,
    ).astype(jnp.bfloat16)
    return (mixed, token_grad, prob_grad, gate_weight_grad, up_weight_grad, down_weight_grad)


def solution(mesh):
    placed = (
        P("dp", "fsdp"),
        P("dp", None),
        P("dp", None),
        P(None, ("dp", "fsdp")),
        P(None, ("dp", "fsdp")),
        P(("dp", "fsdp"), None),
        P("dp", "fsdp"),
    )
    return jax.shard_map(
        local,
        mesh=mesh,
        in_specs=placed,
        out_specs=(
            P("dp", "fsdp"),
            P("dp", "fsdp"),
            P("dp", None),
            P(None, ("dp", "fsdp")),
            P(None, ("dp", "fsdp")),
            P(("dp", "fsdp"), None),
        ),
        check_vma=False,
    )
```

profile of v0, /device:TPU:2, one launch (start us, length us, event | category | flops | bytes accessed | tf_op | source)
XLA Modules:
  0.0 347.4 jit_solution(6366988755404527250)
XLA Ops:
  10.8 24.6 %all-gather.3.cloned.1.call-done = bf16[128,4096]{1,0:T(8,128)(2,1)} async-done(((bf16[128,512]{1,0:T(8,128)(2,1)}), bf16[128,4096]{1,0:T(8,128)(2,1)}) %all-gather.3.cloned.1.call-update) | async-done | bytes 1048592 | tf_op jit(solution)/shard_map/all_gather | solution.py:47
  35.5 2.2 convolution_convert_fusion.5
  37.6 3.0 broadcast_in_dim.27
  40.6 7.5 %all-to-all-start = ((bf16[16,40,4096]{2,1,0:T(8,128)(2,1)}), bf16[16,40,4096]{2,1,0:T(8,128)(2,1)}, u32[]{:S(2)}, u32[]{:S(2)}) async-start(bf16[16,40,4096]{2,1,0:T(8,128)(2,1)} %bitcast.57), calls=%async_computation | async-start | bytes 10485760 | tf_op jit(solution)/shard_map/all_to_all | solution.py:48
  49.0 24.8 %all-gather.5.cloned.1.call-done = bf16[128,4096]{1,0:T(8,128)(2,1)} async-done(((bf16[128,512]{1,0:T(8,128)(2,1)}), bf16[128,4096]{1,0:T(8,128)(2,1)}) %all-gather.5.cloned.1.call-update) | async-done | bytes 1048592 | tf_op jit(solution)/shard_map/all_gather | solution.py:47
  73.8 3.6 %convolution_convert_fusion.4 = bf16[320,4096]{1,0:T(8,128)(2,1)S(1)} fusion(bf16[128,4096]{1,0:T(8,128)(2,1)} %all-gather.5.cloned.1.call-done, f32[128]{0:T(128)S(1)} %get-tuple-element.13, f32[128]{0:T(128)S(1)} %get-tuple-element.12, s32[128]{0:T(128)S(1)} %get-tuple-element.15, s32[128]{0:T(128)S(1)} %get-tuple-element.14), kind=kOutput, calls=%fused_computation.5 | convolution fusion | flops 2014781440 | bytes 3672064 | tf_op jit(solution)/shard_map/dot_general | solution.py:32
  77.4 38.4 %all-to-all-done = bf16[16,40,4096]{2,1,0:T(8,128)(2,1)} async-done(((bf16[16,40,4096]{2,1,0:T(8,128)(2,1)}), bf16[16,40,4096]{2,1,0:T(8,128)(2,1)}, u32[]{:S(2)}, u32[]{:S(2)}) %all-to-all-start) | async-done | bytes 5242912 | tf_op jit(solution)/shard_map/all_to_all | solution.py:48
  115.7 3.0 broadcast_in_dim.31
  118.7 24.0 %all-to-all-start.2 = ((bf16[16,40,4096]{2,1,0:T(8,128)(2,1)}), bf16[16,40,4096]{2,1,0:T(8,128)(2,1)}, u32[]{:S(2)}, u32[]{:S(2)}) async-start(bf16[16,40,4096]{2,1,0:T(8,128)(2,1)} %bitcast.58), calls=%async_computation.3 | async-start | bytes 10485760 | tf_op jit(solution)/shard_map/all_to_all | solution.py:48
  143.0 7.8 %fusion.26 = f32[640,512]{1,0:T(8,128)} fusion(bf16[640,4096]{1,0:T(8,128)(2,1)} %bitcast.7, bf16[4096,512]{1,0:T(8,128)(2,1)} %param.10), kind=kOutput, calls=%fused_computation.53 | convolution fusion | flops 2684354560 | bytes 10747904 | tf_op jit(solution)/shard_map/dot_general | solution.py:69
  150.8 6.4 %fusion.27 = f32[640,512]{1,0:T(8,128)} fusion(bf16[640,4096]{1,0:T(8,128)(2,1)} %bitcast.7, bf16[4096,512]{1,0:T(8,128)(2,1)S(1)} %copy-done.3), kind=kOutput, calls=%fused_computation.54 | convolution fusion | flops 2684354560 | bytes 10747904 | tf_op jit(solution)/shard_map/dot_general | solution.py:70
  157.2 53.1 %all-to-all-done.2 = bf16[16,40,4096]{2,1,0:T(8,128)(2,1)} async-done(((bf16[16,40,4096]{2,1,0:T(8,128)(2,1)}), bf16[16,40,4096]{2,1,0:T(8,128)(2,1)}, u32[]{:S(2)}, u32[]{:S(2)}) %all-to-all-start.2) | async-done | bytes 5242912 | tf_op jit(solution)/shard_map/all_to_all | solution.py:48
  210.3 8.0 %multiply_convert_fusion = (bf16[640,512]{1,0:T(8,128)(2,1)S(1)}, bf16[640,512]{1,0:T(8,128)(2,1)S(1)}, bf16[640,512]{1,0:T(8,128)(2,1)S(1)}) fusion(f32[640,512]{1,0:T(8,128)} %fusion.26, f32[640,512]{1,0:T(8,128)} %fusion.27, bf16[640,4096]{1,0:T(8,128)(2,1)} %bitcast.14, bf16[512,4096]{1,0:T(8,128)(2,1)} %param.12), kind=kOutput, calls=%fused_computation.9 | convolution fusion | flops 2689269760 | bytes 14024704 | tf_op jit(solution)/shard_map/dot_general | solution.py:98
  218.3 4.7 %convolution_convert_fusion = bf16[640,4096]{1,0:T(8,128)(2,1)} fusion(bf16[640,512]{1,0:T(8,128)(2,1)S(1)} %get-tuple-element.10, bf16[512,4096]{1,0:T(8,128)(2,1)S(1)} %copy-done.2), kind=kOutput, calls=%fused_computation.1 | convolution fusion | flops 2686976000 | bytes 10092544 | tf_op jit(solution)/shard_map/dot_general | solution.py:74
  223.3 4.9 %fusion.28 = f32[640,4096]{1,0:T(8,128)S(1)} fusion(bf16[640,512]{1,0:T(8,128)(2,1)S(1)} %get-tuple-element.9, bf16[4096,512]{1,0:T(8,128)(2,1)} %param.10), kind=kOutput, calls=%fused_computation.55 | convolution fusion | flops 2684354560 | bytes 15335424 | tf_op jit(solution)/shard_map/dot_general | solution.py:112
  228.2 4.8 %add_convert_fusion = bf16[640,4096]{1,0:T(8,128)(2,1)} fusion(f32[640,4096]{1,0:T(8,128)S(1)} %fusion.28, bf16[640,512]{1,0:T(8,128)(2,1)S(1)} %get-tuple-element.8, bf16[4096,512]{1,0:T(8,128)(2,1)S(1)} %copy-done.4), kind=kOutput, calls=%fused_computation | convolution fusion | flops 2689597440 | bytes 20578304 | tf_op jit(solution)/shard_map/dot_general | solution.py:115
  233.0 7.5 %convolution_convert_fusion.1 = bf16[512,4096]{1,0:T(8,128)(2,1)} fusion(bf16[640,512]{1,0:T(8,128)(2,1)S(1)} %get-tuple-element.10, bf16[640,4096]{1,0:T(8,128)(2,1)} %bitcast.14), kind=kOutput, calls=%fused_computation.2 | convolution fusion | flops 2686451712 | bytes 10092544 | tf_op jit(solution)/shard_map/dot_general | solution.py:109
  240.5 7.5 %convolution_convert_fusion.2 = bf16[4096,512]{1,0:T(8,128)(2,1)} fusion(bf16[640,4096]{1,0:T(8,128)(2,1)} %bitcast.7, bf16[640,512]{1,0:T(8,128)(2,1)S(1)} %get-tuple-element.8), kind=kOutput, calls=%fused_computation.3 | convolution fusion | flops 2686451712 | bytes 10092544 | tf_op jit(solution)/shard_map/dot_general | solution.py:106
  248.0 26.8 %reduce-scatter.3.cloned.1.call-done = bf16[640,512]{1,0:T(8,128)(2,1)} async-done(((bf16[640,4096]{1,0:T(8,128)(2,1)}), bf16[640,512]{1,0:T(8,128)(2,1)}) %reduce-scatter.3.cloned.1.call-update) | async-done | bytes 655376 | tf_op jit(solution)/shard_map/reduce_scatter | solution.py:54
  274.8 7.5 %all-to-all-start.1 = ((bf16[16,40,512]{2,1,0:T(8,128)(2,1)}), bf16[16,40,512]{2,1,0:T(8,128)(2,1)S(1)}, u32[]{:S(2)}, u32[]{:S(2)}) async-start(bf16[16,40,512]{2,1,0:T(8,128)(2,1)} %bitcast.65), calls=%async_computation.2 | async-start | bytes 1310720 | tf_op jit(solution)/shard_map/all_to_all | solution.py:57
  282.3 7.6 %convolution_convert_fusion.3 = bf16[4096,512]{1,0:T(8,128)(2,1)} fusion(bf16[640,4096]{1,0:T(8,128)(2,1)} %bitcast.7, bf16[640,512]{1,0:T(8,128)(2,1)S(1)} %get-tuple-element.9), kind=kOutput, calls=%fused_computation.4 | convolution fusion | flops 2686451712 | bytes 10092544 | tf_op jit(solution)/shard_map/dot_general | solution.py:103
  289.9 26.6 %reduce-scatter.5.cloned.1.call-done = bf16[640,512]{1,0:T(8,128)(2,1)} async-done(((bf16[640,4096]{1,0:T(8,128)(2,1)}), bf16[640,512]{1,0:T(8,128)(2,1)}) %reduce-scatter.5.cloned.1.call-update) | async-done | bytes 655376 | tf_op jit(solution)/shard_map/reduce_scatter | solution.py:54
  316.5 7.5 %all-to-all-start.3 = ((bf16[16,40,512]{2,1,0:T(8,128)(2,1)}), bf16[16,40,512]{2,1,0:T(8,128)(2,1)S(1)}, u32[]{:S(2)}, u32[]{:S(2)}) async-start(bf16[16,40,512]{2,1,0:T(8,128)(2,1)} %bitcast.64), calls=%async_computation.5 | async-start | bytes 1310720 | tf_op jit(solution)/shard_map/all_to_all | solution.py:57
  325.7 13.9 %psum.7 = f32[128,2]{0,1:T(2,128)} all-reduce(f32[128,2]{0,1:T(2,128)S(1)} %pad_maximum_fusion), channel_id=1, replica_groups=mesh['dp'=16,'fsdp'=8] {'fsdp'}, use_global_device_ids=true, to_apply=%region_9.10 | all-reduce | flops 256 | bytes 2048 | tf_op jit(solution)/shard_map/psum | solution.py:96
  (40 shorter events, 7.8 us)
Async XLA Ops:
  7.2 28.3 %all-gather.3.cloned.1.call-start = ((), (), s32[]{:S(2)}) async-start(), calls=%async_computation.6 | async-start | bytes 1179648 | tf_op jit(solution)/shard_map/all_gather | solution.py:47
  40.6 8.3 %copy-start.1 = (f32[128,2]{0,1:T(2,128)S(1)}, f32[128,2]{0,1:T(2,128)}, u32[]{:S(2)}) copy-start(f32[128,2]{0,1:T(2,128)} %param.9) | copy-start | bytes 3076
  40.6 75.1 %all-to-all-start = ((bf16[16,40,4096]{2,1,0:T(8,128)(2,1)}), bf16[16,40,4096]{2,1,0:T(8,128)(2,1)}, u32[]{:S(2)}, u32[]{:S(2)}) async-start(bf16[16,40,4096]{2,1,0:T(8,128)(2,1)} %bitcast.57), calls=%async_computation | async-start | bytes 10485760 | tf_op jit(solution)/shard_map/all_to_all | solution.py:48
  48.2 25.6 %all-gather.5.cloned.1.call-start = ((), (), s32[]{:S(2)}) async-start(), calls=%async_computation.8 | async-start | bytes 1179648 | tf_op jit(solution)/shard_map/all_gather | solution.py:47
  118.7 91.6 %all-to-all-start.2 = ((bf16[16,40,4096]{2,1,0:T(8,128)(2,1)}), bf16[16,40,4096]{2,1,0:T(8,128)(2,1)}, u32[]{:S(2)}, u32[]{:S(2)}) async-start(bf16[16,40,4096]{2,1,0:T(8,128)(2,1)} %bitcast.58), calls=%async_computation.3 | async-start | bytes 10485760 | tf_op jit(solution)/shard_map/all_to_all | solution.py:48
  142.7 132.1 %reduce-scatter.3.cloned.1.call-start = ((), (), s32[]{:S(2)}) async-start(), calls=%async_computation.7 | async-start | bytes 5898240 | tf_op jit(solution)/shard_map/reduce_scatter | solution.py:54
  142.9 7.8 %copy-start.3 = (bf16[4096,512]{1,0:T(8,128)(2,1)S(1)}, bf16[4096,512]{1,0:T(8,128)(2,1)}, u32[]{:S(2)}) copy-start(bf16[4096,512]{1,0:T(8,128)(2,1)} %param.11) | copy-start | bytes 12582916
  210.3 8.0 %copy-start.2 = (bf16[512,4096]{1,0:T(8,128)(2,1)S(1)}, bf16[512,4096]{1,0:T(8,128)(2,1)}, u32[]{:S(2)}) copy-start(bf16[512,4096]{1,0:T(8,128)(2,1)} %param.12) | copy-start | bytes 12582916
  223.0 93.5 %reduce-scatter.5.cloned.1.call-start = ((), (), s32[]{:S(2)}) async-start(), calls=%async_computation.9 | async-start | bytes 5898240 | tf_op jit(solution)/shard_map/reduce_scatter | solution.py:54
  223.3 4.9 %copy-start.4 = (bf16[4096,512]{1,0:T(8,128)(2,1)S(1)}, bf16[4096,512]{1,0:T(8,128)(2,1)}, u32[]{:S(2)}) copy-start(bf16[4096,512]{1,0:T(8,128)(2,1)} %param.11) | copy-start | bytes 12582916
  274.8 41.7 %all-to-all-start.1 = ((bf16[16,40,512]{2,1,0:T(8,128)(2,1)}), bf16[16,40,512]{2,1,0:T(8,128)(2,1)S(1)}, u32[]{:S(2)}, u32[]{:S(2)}) async-start(bf16[16,40,512]{2,1,0:T(8,128)(2,1)} %bitcast.65), calls=%async_computation.2 | async-start | bytes 1310720 | tf_op jit(solution)/shard_map/all_to_all | solution.py:57
  282.2 42.3 %copy-start = (bf16[128,512]{1,0:T(8,128)(2,1)S(1)}, bf16[128,512]{1,0:T(8,128)(2,1)}, u32[]{:S(2)}) copy-start(bf16[128,512]{1,0:T(8,128)(2,1)} %param.13) | copy-start | bytes 393220
  316.5 23.1 %all-to-all-start.3 = ((bf16[16,40,512]{2,1,0:T(8,128)(2,1)}), bf16[16,40,512]{2,1,0:T(8,128)(2,1)S(1)}, u32[]{:S(2)}, u32[]{:S(2)}) async-start(bf16[16,40,512]{2,1,0:T(8,128)(2,1)} %bitcast.64), calls=%async_computation.5 | async-start | bytes 1310720 | tf_op jit(solution)/shard_map/all_to_all | solution.py:57
Sparse Core Ops, SparseCore 0:
  9.7 25.7 all-gather.2
  50.7 23.0 all-gather.4
  223.1 51.6 reduce-scatter.2
  277.0 39.3 reduce-scatter.4
where the time goes:
time: 348 us; the launch traced here: 347 us
  waiting for transfers between devices  196 us (56%)
  matrix products  67.6 us (19%)
  starting transfers between devices  47 us (14%)
  blocking collectives  13.9 us (4%)
  between operations  13.9 us (4%)
  local copies, waits for them, and re-layouts  7.52 us (2%)
    all_to_all x2, waiting for transfers between devices, to_expert_layout(): lax.all_to_all(place_rows(joined, scaled), 'dp', split_axis=0, concat_axi...  91.5 us
    reduce_scatter x2, waiting for transfers between devices, to_token_layout(): lax.psum_scatter(partial_value.astype(jnp.bfloat16), 'fsdp', scatter_dime...  53.4 us
    all_gather x2, waiting for transfers between devices, to_expert_layout(): joined = lax.all_gather(source, 'fsdp', axis=1, tiled=True)  49.5 us
    all_to_all x2, starting transfers between devices, to_expert_layout(): lax.all_to_all(place_rows(joined, scaled), 'dp', split_axis=0, concat_axi...  31.5 us
    all_to_all x2, starting transfers between devices, to_token_layout(): lax.all_to_all(shares.reshape(dp_count, CAP, shares.shape[1]).astype(jnp....  15 us
    psum x1, blocking collectives, local(): prob_grad = lax.psum(prob_terms, 'fsdp')  13.9 us
    dot_general x1, matrix products, local(): lax.dot_general(grad_rows, w_down, back_dims, preferred_element_type=jnp....  7.96 us
    dot_general x1, matrix products, local(): gate_proj = jnp.dot(expert_rows, w_gate, preferred_element_type=jnp.float32)  7.81 us
  transfers between devices with their start and end apart: 8, of which 6 were waited for; matrix products, arithmetic and copies ran while one was open for 16% of the time, Pallas kernels for 0%

commit v1 on v0

--- a/solution.py
+++ b/solution.py
@@ -93,7 +93,7 @@
         [jnp.sum(first_pair * grad_local, axis=1), jnp.sum(second_pair * grad_local, axis=1)],
         axis=1,
     )
-    prob_grad = lax.psum(prob_terms, "fsdp")
+    prob_grad = jnp.sum(lax.all_gather(prob_terms, "fsdp"), axis=0)
     grad_rows = to_expert_layout(out_grad, True)
     hidden_grad = lax.dot_general(grad_rows, w_down, back_dims, preferred_element_type=jnp.float32)
     gate_grad = (

time: 348 us -> 343 us (0.986)
  blocking collectives: 13.9 us -> 7.84 us
    psum x1 -> x0, blocking collectives: 13.9 us -> none  [local(): prob_grad = lax.psum(prob_terms, 'fsdp')]
    all_gather x0 -> x1, blocking collectives: none -> 7.84 us  [local(): prob_grad = jnp.sum(lax.all_gather(prob_terms, 'fsdp'), axis=0)]
where the time goes in v1:
time: 343 us; the launch traced here: 342 us
  waiting for transfers between devices  196 us (57%)
  matrix products  67.6 us (20%)
  starting transfers between devices  47 us (14%)
  between operations  13.9 us (4%)
  blocking collectives  7.84 us (2%)
  local copies, waits for them, and re-layouts  7.52 us (2%)
    all_to_all x2, waiting for transfers between devices, to_expert_layout(): lax.all_to_all(place_rows(joined, scaled), 'dp', split_axis=0, concat_axi...  91.5 us
    reduce_scatter x2, waiting for transfers between devices, to_token_layout(): lax.psum_scatter(partial_value.astype(jnp.bfloat16), 'fsdp', scatter_dime...  53.4 us
    all_gather x2, waiting for transfers between devices, to_expert_layout(): joined = lax.all_gather(source, 'fsdp', axis=1, tiled=True)  49.5 us
    all_to_all x2, starting transfers between devices, to_expert_layout(): lax.all_to_all(place_rows(joined, scaled), 'dp', split_axis=0, concat_axi...  31.5 us
    all_to_all x2, starting transfers between devices, to_token_layout(): lax.all_to_all(shares.reshape(dp_count, CAP, shares.shape[1]).astype(jnp....  15 us
    dot_general x1, matrix products, local(): lax.dot_general(grad_rows, w_down, back_dims, preferred_element_type=jnp....  7.96 us
    all_gather x1, blocking collectives, local(): prob_grad = jnp.sum(lax.all_gather(prob_terms, 'fsdp'), axis=0)  7.84 us
    dot_general x1, matrix products, local(): gate_proj = jnp.dot(expert_rows, w_gate, preferred_element_type=jnp.float32)  7.81 us
  transfers between devices with their start and end apart: 8, of which 6 were waited for; matrix products, arithmetic and copies ran while one was open for 16% of the time, Pallas kernels for 0%

profile of v1, /device:TPU:2, one launch (start us, length us, event | category | flops | bytes accessed | tf_op | source)
XLA Modules:
  0.0 341.9 jit_solution(956578498228259277)
XLA Ops:
  10.8 24.6 %all-gather.4.cloned.1.call-done = bf16[128,4096]{1,0:T(8,128)(2,1)} async-done(((bf16[128,512]{1,0:T(8,128)(2,1)}), bf16[128,4096]{1,0:T(8,128)(2,1)}) %all-gather.4.cloned.1.call-update) | async-done | bytes 1048592 | tf_op jit(solution)/shard_map/all_gather | solution.py:47
  35.5 2.2 convolution_convert_fusion.5
  37.6 3.0 broadcast_in_dim.27
  40.6 7.5 %all-to-all-start = ((bf16[16,40,4096]{2,1,0:T(8,128)(2,1)}), bf16[16,40,4096]{2,1,0:T(8,128)(2,1)}, u32[]{:S(2)}, u32[]{:S(2)}) async-start(bf16[16,40,4096]{2,1,0:T(8,128)(2,1)} %bitcast.62), calls=%async_computation | async-start | bytes 10485760 | tf_op jit(solution)/shard_map/all_to_all | solution.py:48
  49.0 24.8 %all-gather.6.cloned.1.call-done = bf16[128,4096]{1,0:T(8,128)(2,1)} async-done(((bf16[128,512]{1,0:T(8,128)(2,1)}), bf16[128,4096]{1,0:T(8,128)(2,1)}) %all-gather.6.cloned.1.call-update) | async-done | bytes 1048592 | tf_op jit(solution)/shard_map/all_gather | solution.py:47
  73.8 3.6 %convolution_convert_fusion.4 = bf16[320,4096]{1,0:T(8,128)(2,1)S(1)} fusion(bf16[128,4096]{1,0:T(8,128)(2,1)} %all-gather.6.cloned.1.call-done, f32[128]{0:T(128)S(1)} %get-tuple-element.13, f32[128]{0:T(128)S(1)} %get-tuple-element.12, s32[128]{0:T(128)S(1)} %get-tuple-element.15, s32[128]{0:T(128)S(1)} %get-tuple-element.14), kind=kOutput, calls=%fused_computation.5 | convolution fusion | flops 2014781440 | bytes 3672064 | tf_op jit(solution)/shard_map/dot_general | solution.py:32
  77.4 38.4 %all-to-all-done = bf16[16,40,4096]{2,1,0:T(8,128)(2,1)} async-done(((bf16[16,40,4096]{2,1,0:T(8,128)(2,1)}), bf16[16,40,4096]{2,1,0:T(8,128)(2,1)}, u32[]{:S(2)}, u32[]{:S(2)}) %all-to-all-start) | async-done | bytes 5242912 | tf_op jit(solution)/shard_map/all_to_all | solution.py:48
  115.7 3.0 broadcast_in_dim.31
  118.7 24.0 %all-to-all-start.2 = ((bf16[16,40,4096]{2,1,0:T(8,128)(2,1)}), bf16[16,40,4096]{2,1,0:T(8,128)(2,1)}, u32[]{:S(2)}, u32[]{:S(2)}) async-start(bf16[16,40,4096]{2,1,0:T(8,128)(2,1)} %bitcast.63), calls=%async_computation.3 | async-start | bytes 10485760 | tf_op jit(solution)/shard_map/all_to_all | solution.py:48
  143.0 7.8 %fusion.26 = f32[640,512]{1,0:T(8,128)} fusion(bf16[640,4096]{1,0:T(8,128)(2,1)} %bitcast.7, bf16[4096,512]{1,0:T(8,128)(2,1)} %param.10), kind=kOutput, calls=%fused_computation.54 | convolution fusion | flops 2684354560 | bytes 10747904 | tf_op jit(solution)/shard_map/dot_general | solution.py:69
  150.8 6.4 %fusion.27 = f32[640,512]{1,0:T(8,128)} fusion(bf16[640,4096]{1,0:T(8,128)(2,1)} %bitcast.7, bf16[4096,512]{1,0:T(8,128)(2,1)S(1)} %copy-done.3), kind=kOutput, calls=%fused_computation.55 | convolution fusion | flops 2684354560 | bytes 10747904 | tf_op jit(solution)/shard_map/dot_general | solution.py:70
  157.2 53.1 %all-to-all-done.2 = bf16[16,40,4096]{2,1,0:T(8,128)(2,1)} async-done(((bf16[16,40,4096]{2,1,0:T(8,128)(2,1)}), bf16[16,40,4096]{2,1,0:T(8,128)(2,1)}, u32[]{:S(2)}, u32[]{:S(2)}) %all-to-all-start.2) | async-done | bytes 5242912 | tf_op jit(solution)/shard_map/all_to_all | solution.py:48
  210.3 8.0 %multiply_convert_fusion = (bf16[640,512]{1,0:T(8,128)(2,1)S(1)}, bf16[640,512]{1,0:T(8,128)(2,1)S(1)}, bf16[640,512]{1,0:T(8,128)(2,1)S(1)}) fusion(f32[640,512]{1,0:T(8,128)} %fusion.26, f32[640,512]{1,0:T(8,128)} %fusion.27, bf16[640,4096]{1,0:T(8,128)(2,1)} %bitcast.14, bf16[512,4096]{1,0:T(8,128)(2,1)} %param.12), kind=kOutput, calls=%fused_computation.9 | convolution fusion | flops 2689269760 | bytes 14024704 | tf_op jit(solution)/shard_map/dot_general | solution.py:98
  218.3 4.7 %convolution_convert_fusion = bf16[640,4096]{1,0:T(8,128)(2,1)} fusion(bf16[640,512]{1,0:T(8,128)(2,1)S(1)} %get-tuple-element.10, bf16[512,4096]{1,0:T(8,128)(2,1)S(1)} %copy-done.2), kind=kOutput, calls=%fused_computation.1 | convolution fusion | flops 2686976000 | bytes 10092544 | tf_op jit(solution)/shard_map/dot_general | solution.py:74
  223.3 4.9 %fusion.28 = f32[640,4096]{1,0:T(8,128)S(1)} fusion(bf16[640,512]{1,0:T(8,128)(2,1)S(1)} %get-tuple-element.9, bf16[4096,512]{1,0:T(8,128)(2,1)} %param.10), kind=kOutput, calls=%fused_computation.56 | convolution fusion | flops 2684354560 | bytes 15335424 | tf_op jit(solution)/shard_map/dot_general | solution.py:112
  228.2 4.8 %add_convert_fusion = bf16[640,4096]{1,0:T(8,128)(2,1)} fusion(f32[640,4096]{1,0:T(8,128)S(1)} %fusion.28, bf16[640,512]{1,0:T(8,128)(2,1)S(1)} %get-tuple-element.8, bf16[4096,512]{1,0:T(8,128)(2,1)S(1)} %copy-done.4), kind=kOutput, calls=%fused_computation | convolution fusion | flops 2689597440 | bytes 20578304 | tf_op jit(solution)/shard_map/dot_general | solution.py:115
  233.0 7.5 %convolution_convert_fusion.1 = bf16[512,4096]{1,0:T(8,128)(2,1)} fusion(bf16[640,512]{1,0:T(8,128)(2,1)S(1)} %get-tuple-element.10, bf16[640,4096]{1,0:T(8,128)(2,1)} %bitcast.14), kind=kOutput, calls=%fused_computation.2 | convolution fusion | flops 2686451712 | bytes 10092544 | tf_op jit(solution)/shard_map/dot_general | solution.py:109
  240.5 7.5 %convolution_convert_fusion.2 = bf16[4096,512]{1,0:T(8,128)(2,1)} fusion(bf16[640,4096]{1,0:T(8,128)(2,1)} %bitcast.7, bf16[640,512]{1,0:T(8,128)(2,1)S(1)} %get-tuple-element.8), kind=kOutput, calls=%fused_computation.3 | convolution fusion | flops 2686451712 | bytes 10092544 | tf_op jit(solution)/shard_map/dot_general | solution.py:106
  248.0 26.8 %reduce-scatter.3.cloned.1.call-done = bf16[640,512]{1,0:T(8,128)(2,1)} async-done(((bf16[640,4096]{1,0:T(8,128)(2,1)}), bf16[640,512]{1,0:T(8,128)(2,1)}) %reduce-scatter.3.cloned.1.call-update) | async-done | bytes 655376 | tf_op jit(solution)/shard_map/reduce_scatter | solution.py:54
  274.8 7.5 %all-to-all-start.1 = ((bf16[16,40,512]{2,1,0:T(8,128)(2,1)}), bf16[16,40,512]{2,1,0:T(8,128)(2,1)S(1)}, u32[]{:S(2)}, u32[]{:S(2)}) async-start(bf16[16,40,512]{2,1,0:T(8,128)(2,1)} %bitcast.70), calls=%async_computation.2 | async-start | bytes 1310720 | tf_op jit(solution)/shard_map/all_to_all | solution.py:57
  282.3 7.6 %convolution_convert_fusion.3 = bf16[4096,512]{1,0:T(8,128)(2,1)} fusion(bf16[640,4096]{1,0:T(8,128)(2,1)} %bitcast.7, bf16[640,512]{1,0:T(8,128)(2,1)S(1)} %get-tuple-element.9), kind=kOutput, calls=%fused_computation.4 | convolution fusion | flops 2686451712 | bytes 10092544 | tf_op jit(solution)/shard_map/dot_general | solution.py:103
  289.9 26.6 %reduce-scatter.5.cloned.1.call-done = bf16[640,512]{1,0:T(8,128)(2,1)} async-done(((bf16[640,4096]{1,0:T(8,128)(2,1)}), bf16[640,512]{1,0:T(8,128)(2,1)}) %reduce-scatter.5.cloned.1.call-update) | async-done | bytes 655376 | tf_op jit(solution)/shard_map/reduce_scatter | solution.py:54
  316.5 7.5 %all-to-all-start.3 = ((bf16[16,40,512]{2,1,0:T(8,128)(2,1)}), bf16[16,40,512]{2,1,0:T(8,128)(2,1)S(1)}, u32[]{:S(2)}, u32[]{:S(2)}) async-start(bf16[16,40,512]{2,1,0:T(8,128)(2,1)} %bitcast.69), calls=%async_computation.5 | async-start | bytes 1310720 | tf_op jit(solution)/shard_map/all_to_all | solution.py:57
  325.7 7.8 %all-gather = f32[1024,2]{0,1:T(2,128)S(1)} all-gather(f32[128,2]{0,1:T(2,128)S(1)} %pad_maximum_fusion), channel_id=2, replica_groups=mesh['dp'=16,'fsdp'=8] {'fsdp'}, dimensions={0}, use_global_device_ids=true | all-gather | bytes 9216 | tf_op jit(solution)/shard_map/all_gather | solution.py:96
  (41 shorter events, 8.4 us)
Async XLA Ops:
  7.2 28.3 %all-gather.4.cloned.1.call-start = ((), (), s32[]{:S(2)}) async-start(), calls=%async_computation.6 | async-start | bytes 1179648 | tf_op jit(solution)/shard_map/all_gather | solution.py:47
  40.6 8.3 %copy-start.1 = (f32[128,2]{0,1:T(2,128)S(1)}, f32[128,2]{0,1:T(2,128)}, u32[]{:S(2)}) copy-start(f32[128,2]{0,1:T(2,128)} %param.9) | copy-start | bytes 3076
  40.6 75.1 %all-to-all-start = ((bf16[16,40,4096]{2,1,0:T(8,128)(2,1)}), bf16[16,40,4096]{2,1,0:T(8,128)(2,1)}, u32[]{:S(2)}, u32[]{:S(2)}) async-start(bf16[16,40,4096]{2,1,0:T(8,128)(2,1)} %bitcast.62), calls=%async_computation | async-start | bytes 10485760 | tf_op jit(solution)/shard_map/all_to_all | solution.py:48
  48.2 25.6 %all-gather.6.cloned.1.call-start = ((), (), s32[]{:S(2)}) async-start(), calls=%async_computation.8 | async-start | bytes 1179648 | tf_op jit(solution)/shard_map/all_gather | solution.py:47
  118.7 91.6 %all-to-all-start.2 = ((bf16[16,40,4096]{2,1,0:T(8,128)(2,1)}), bf16[16,40,4096]{2,1,0:T(8,128)(2,1)}, u32[]{:S(2)}, u32[]{:S(2)}) async-start(bf16[16,40,4096]{2,1,0:T(8,128)(2,1)} %bitcast.63), calls=%async_computation.3 | async-start | bytes 10485760 | tf_op jit(solution)/shard_map/all_to_all | solution.py:48
  142.7 132.1 %reduce-scatter.3.cloned.1.call-start = ((), (), s32[]{:S(2)}) async-start(), calls=%async_computation.7 | async-start | bytes 5898240 | tf_op jit(solution)/shard_map/reduce_scatter | solution.py:54
  142.9 7.8 %copy-start.3 = (bf16[4096,512]{1,0:T(8,128)(2,1)S(1)}, bf16[4096,512]{1,0:T(8,128)(2,1)}, u32[]{:S(2)}) copy-start(bf16[4096,512]{1,0:T(8,128)(2,1)} %param.11) | copy-start | bytes 12582916
  210.3 8.0 %copy-start.2 = (bf16[512,4096]{1,0:T(8,128)(2,1)S(1)}, bf16[512,4096]{1,0:T(8,128)(2,1)}, u32[]{:S(2)}) copy-start(bf16[512,4096]{1,0:T(8,128)(2,1)} %param.12) | copy-start | bytes 12582916
  223.0 93.5 %reduce-scatter.5.cloned.1.call-start = ((), (), s32[]{:S(2)}) async-start(), calls=%async_computation.9 | async-start | bytes 5898240 | tf_op jit(solution)/shard_map/reduce_scatter | solution.py:54
  223.3 4.9 %copy-start.4 = (bf16[4096,512]{1,0:T(8,128)(2,1)S(1)}, bf16[4096,512]{1,0:T(8,128)(2,1)}, u32[]{:S(2)}) copy-start(bf16[4096,512]{1,0:T(8,128)(2,1)} %param.11) | copy-start | bytes 12582916
  274.8 41.7 %all-to-all-start.1 = ((bf16[16,40,512]{2,1,0:T(8,128)(2,1)}), bf16[16,40,512]{2,1,0:T(8,128)(2,1)S(1)}, u32[]{:S(2)}, u32[]{:S(2)}) async-start(bf16[16,40,512]{2,1,0:T(8,128)(2,1)} %bitcast.70), calls=%async_computation.2 | async-start | bytes 1310720 | tf_op jit(solution)/shard_map/all_to_all | solution.py:57
  282.2 42.3 %copy-start = (bf16[128,512]{1,0:T(8,128)(2,1)S(1)}, bf16[128,512]{1,0:T(8,128)(2,1)}, u32[]{:S(2)}) copy-start(bf16[128,512]{1,0:T(8,128)(2,1)} %param.13) | copy-start | bytes 393220
  316.5 17.6 %all-to-all-start.3 = ((bf16[16,40,512]{2,1,0:T(8,128)(2,1)}), bf16[16,40,512]{2,1,0:T(8,128)(2,1)S(1)}, u32[]{:S(2)}, u32[]{:S(2)}) async-start(bf16[16,40,512]{2,1,0:T(8,128)(2,1)} %bitcast.69), calls=%async_computation.5 | async-start | bytes 1310720 | tf_op jit(solution)/shard_map/all_to_all | solution.py:57
Sparse Core Ops, SparseCore 0:
  9.7 25.7 all-gather.3
  50.7 23.0 all-gather.5
  223.1 51.6 reduce-scatter.2
  277.0 39.3 reduce-scatter.4
